TPU v7x, 128 devices: a whole 4x4x4 slice. The times are simulated.
128 devices in a mesh: seq: 128 (over y, x, z, core).
Axes of the slice: x: 4, y: 4, z: 4, core: 2. Of those that a mesh axis runs over, the one named last changes fastest.
Arguments:
- queries: bfloat16 [16384, 8192], P('seq'), may hold values from -5.1 to 5.1
- keys: bfloat16 [16384, 1024], P('seq'), may hold values from -5.1 to 5.1
- values: bfloat16 [16384, 1024], P('seq'), may hold values from -6 to 6
- lengths: int32 [32], replicated, may hold values from 1 to 8, 128 in all
- class_weight: bfloat16 [8192, 16], replicated, may hold values from -0.25 to 0.25
Outputs:
- attended: bfloat16 [16384, 8192], P('seq')
- doc_logits: float32 [128, 16], P('seq')
Inputs may be any that keep to these rules, and one draw needn't show every extreme that they name: `lengths`: lengths are counted in blocks of 128 tokens; they sum to 128 and the longest is exactly 8 blocks.
All inputs are finite; a program needn't handle non-finite values.
Results may differ from a plain program's by a relative error of at most 0.0046.
Values may be sent and summed in bfloat16 or wider, within the bound.
No kernel may reach another device: no remote copies, remote signals or barrier semaphores. Data moves between devices by JAX's collectives and lax.ppermute only.
A program may use at most 192 MiB of HBM per device.

v0:
```python
import jax
import jax.numpy as jnp
from jax import lax
from jax.sharding import PartitionSpec as P
from jax.experimental import pallas as pl
from jax.experimental.pallas import tpu as pltpu

DH = 128
BLK = 128
MAXB = 8


def shifted(block, axis, distance):
    count = lax.axis_size(axis)
    if distance > 0:
        route = [(i - distance, i) for i in range(distance, count)]
    else:
        route = [(i - distance, i) for i in range(0, count + distance)]
    return lax.ppermute(block, axis, route)


def block_docs(lengths, block_count):
    doc_ends = jnp.cumsum(lengths, dtype=jnp.int32)
    doc_firsts = doc_ends - lengths
    blocks = jnp.arange(block_count, dtype=jnp.int32)
    owner_doc = jnp.sum((doc_ends[None, :] <= blocks[:, None]).astype(jnp.int32), axis=1)
    matches = owner_doc[:, None] == jnp.arange(lengths.shape[0], dtype=jnp.int32)[None, :]
    first_block = jnp.sum(jnp.where(matches, doc_firsts[None, :], 0), axis=1)
    return (owner_doc, first_block)


def attention_kernel(flags_ref, q_ref, q0t_ref, stack_ref, *refs):
    own = len(refs) - 9
    out_ref, out0_ref, qt_ref, m_ref, l_ref, acc_ref, m0_ref, l0_ref, acc0_ref = refs[own:]
    loaders = [lambda cols, r=r: r[0 : q_ref.shape[1], cols] for r in refs[:own]]
    loaders += [
        lambda cols, i=i: stack_ref[i, 0 : q_ref.shape[1], cols] for i in range(stack_ref.shape[0])
    ]
    heads = q_ref.shape[0]
    rows = q_ref.shape[1]
    width_k = stack_ref.shape[2] // 2
    heads_kv = width_k // DH
    group = heads // heads_kv
    factor = DH ** (-0.5)

    def prep(j, carry):
        qt_ref[j] = q_ref[j].astype(jnp.float32).T.astype(jnp.bfloat16)
        return carry

    lax.fori_loop(0, heads, prep, 0)

    def merge(first, ms, ls, accs, j, m1, l1, o1):
        if first:
            ms[j] = m1
            ls[j] = l1
            accs[j] = o1
        else:
            m0 = ms[j]
            mn = jnp.maximum(m0, m1)
            a = jnp.exp(m0 - mn)
            b = jnp.exp(m1 - mn)
            ms[j] = mn
            ls[j] = ls[j] * a + l1 * b
            accs[j] = accs[j] * a + o1 * b

    def scored(k, vt, qt):
        st = jnp.dot(k, qt, preferred_element_type=jnp.float32) * factor
        m1 = jnp.max(st, axis=0, keepdims=True)
        p = jnp.exp(st - m1)
        l1 = jnp.sum(p, axis=0, keepdims=True)
        ot = jnp.dot(vt, p.astype(jnp.bfloat16), preferred_element_type=jnp.float32)
        return m1, l1, ot

    def tile_step(load, first):
        def one_head(h, carry):
            kcol = pl.multiple_of(h * DH, DH)
            vcol = pl.multiple_of(width_k + h * DH, DH)
            k = load(pl.ds(kcol, DH))
            vt = load(pl.ds(vcol, DH)).astype(jnp.float32).T.astype(jnp.bfloat16)
            for g in range(group):
                j = h * group + g
                merge(first, m_ref, l_ref, acc_ref, j, *scored(k, vt, qt_ref[j]))
            merge(first, m0_ref, l0_ref, acc0_ref, h, *scored(k, vt, q0t_ref[h]))
            return carry

        lax.fori_loop(0, heads_kv, one_head, 0)

    tile_step(loaders[0], True)
    for t in range(1, len(loaders)):

        @pl.when(flags_ref[t] > 0)
        def _(load=loaders[t]):
            tile_step(load, False)

    def finish(j, carry):
        col = pl.multiple_of(j * DH, DH)
        out_ref[:, pl.ds(col, DH)] = (acc_ref[j] / l_ref[j]).T.astype(out_ref.dtype)
        return carry

    lax.fori_loop(0, heads, finish, 0)
    for h in range(heads_kv):
        out0_ref[h] = acc0_ref[h] / l0_ref[h]


def attend(flags, q_heads, q0t, partner_stack, pieces):
    heads, rows, _ = q_heads.shape
    heads_kv = q0t.shape[0]
    width = q0t.shape[2]
    return pl.pallas_call(
        attention_kernel,
        out_shape=(
            jax.ShapeDtypeStruct((rows, heads * DH), jnp.bfloat16),
            jax.ShapeDtypeStruct((heads_kv, DH, width), jnp.float32),
        ),
        in_specs=[pl.BlockSpec(memory_space=pltpu.SMEM)]
        + [pl.BlockSpec(memory_space=pltpu.VMEM)] * (3 + len(pieces)),
        out_specs=(pl.BlockSpec(memory_space=pltpu.VMEM), pl.BlockSpec(memory_space=pltpu.VMEM)),
        scratch_shapes=[
            pltpu.VMEM((heads, DH, rows), jnp.bfloat16),
            pltpu.VMEM((heads, 1, rows), jnp.float32),
            pltpu.VMEM((heads, 1, rows), jnp.float32),
            pltpu.VMEM((heads, DH, rows), jnp.float32),
            pltpu.VMEM((heads_kv, 1, width), jnp.float32),
            pltpu.VMEM((heads_kv, 1, width), jnp.float32),
            pltpu.VMEM((heads_kv, DH, width), jnp.float32),
        ],
        compiler_params=pltpu.CompilerParams(vmem_limit_bytes=56 * 1024 * 1024),
    )(flags, q_heads, q0t, partner_stack, *pieces)


def shards(queries, keys, values, lengths, class_weight):
    devices = lax.axis_size("seq")
    myself = lax.axis_index("seq")
    row_count = queries.shape[0]
    width_q = queries.shape[1]
    width_k = keys.shape[1]
    heads = width_q // DH
    heads_kv = width_k // DH
    group = heads // heads_kv
    arrived_q = lax.all_to_all(
        queries.reshape(devices, heads, DH), "seq", split_axis=0, concat_axis=0, tiled=True
    )
    arrived_kv = lax.all_to_all(
        jnp.concatenate(
            [keys.reshape(devices, heads_kv, DH), values.reshape(devices, heads_kv, DH)], axis=1
        ),
        "seq",
        split_axis=0,
        concat_axis=0,
        tiled=True,
    )
    q_heads = arrived_q.transpose(1, 0, 2)
    own_q0 = arrived_q[0].reshape(-1, 2 * width_k)
    kv = jnp.concatenate([arrived_kv.reshape(row_count, 2 * width_k), own_q0], axis=0)
    owner_doc, first_block = block_docs(lengths, devices)
    my_doc = owner_doc[myself]
    partner = myself + 1 - 2 * (myself % 2)
    pieces = [kv]
    offsets = [0]
    right = kv
    left = kv
    for hop in range(1, MAXB // 2 + 1):
        right = shifted(right, "seq", 2)
        left = shifted(left, "seq", -2)
        pieces += [right, left]
        offsets += [-2 * hop, 2 * hop]
    partner_stack = lax.ppermute(
        jnp.stack(pieces), "seq", [(i, i + 1 - 2 * (i % 2)) for i in range(devices)]
    )
    offsets = jnp.array(offsets, jnp.int32)
    blocks = jnp.concatenate([myself + offsets, partner + offsets])
    inside = (blocks >= 0) & (blocks < devices)
    docs = jnp.take(owner_doc, jnp.clip(blocks, 0, devices - 1))
    flags = (inside & (docs == my_doc)).astype(jnp.int32).at[0].set(1)
    firsts = jnp.concatenate(
        [jnp.stack([p[row_count:] for p in pieces]), partner_stack[:, row_count:]], axis=0
    )
    picked = (blocks == first_block[myself]).astype(firsts.dtype)
    start_q0 = jnp.sum(firsts * picked[:, None, None], axis=0).astype(firsts.dtype)
    q0t = start_q0.reshape(heads_kv, group, DH).transpose(0, 2, 1)
    q0t = jnp.pad(q0t, ((0, 0), (0, 0), (0, DH - group)))
    attended, start_out = attend(flags, q_heads, q0t, partner_stack, pieces)
    start_row = start_out[:, :, :group].transpose(0, 2, 1).reshape(1, width_q).astype(jnp.bfloat16)
    doc_logits = jnp.dot(start_row, class_weight, preferred_element_type=jnp.float32)
    return (attended, doc_logits)


def solution(mesh):
    return jax.shard_map(
        shards,
        mesh=mesh,
        in_specs=(P("seq", None), P("seq", None), P("seq", None), P(), P()),
        out_specs=(P("seq", None), P("seq", None)),
        check_vma=False,
    )
```

profile of v0, /device:TPU:17, one launch (start us, length us, event | category | flops | bytes accessed | tf_op | source)
XLA Modules:
  0.0 208.1 jit_solution(10401590000200748578)
XLA Ops:
  0.6 1.0 copy.26
  3.6 10.6 %all-to-all-start.1 = ((bf16[128,16,128]{2,1,0:T(8,128)(2,1)}), bf16[128,16,128]{2,1,0:T(8,128)(2,1)S(1)}, u32[]{:S(2)}, u32[]{:S(2)}) async-start(bf16[128,16,128]{2,1,0:T(8,128)(2,1)} %pad_maximum_fusion), calls=%async_computation.1 | async-start | bytes 1048576 | tf_op jit(solution)/shard_map/all_to_all | solution.py:143
  14.2 3.2 %copy.21 = bf16[128,8192]{0,1:T(8,128)(2,1)S(1)} copy(bf16[128,8192]{1,0:T(8,128)(2,1)} %param.8) | data formatting | bytes 4194304 | tf_op args[0]
  17.4 2.8 %copy.22 = bf16[128,64,128]{2,1,0:T(8,128)(2,1)} copy(bf16[128,64,128]{0,2,1:T(8,128)(2,1)S(1)} %bitcast.77) | data formatting | bytes 4194304 | tf_op jit(solution)/shard_map/reshape | solution.py:141
  20.2 5.7 %all-to-all-done.1 = bf16[128,16,128]{2,1,0:T(8,128)(2,1)S(1)} async-done(((bf16[128,16,128]{2,1,0:T(8,128)(2,1)}), bf16[128,16,128]{2,1,0:T(8,128)(2,1)S(1)}, u32[]{:S(2)}, u32[]{:S(2)}) %all-to-all-start.1) | async-done | bytes 524320 | tf_op jit(solution)/shard_map/all_to_all | solution.py:143
  25.9 6.7 %all-to-all-start = ((bf16[128,64,128]{2,1,0:T(8,128)(2,1)}), bf16[128,64,128]{2,1,0:T(8,128)(2,1)S(1)}, u32[]{:S(2)}, u32[]{:S(2)}) async-start(bf16[128,64,128]{2,1,0:T(8,128)(2,1)} %copy.22), calls=%async_computation | async-start | bytes 4194304 | tf_op jit(solution)/shard_map/all_to_all | solution.py:140
  32.6 28.3 %all-to-all-done = bf16[128,64,128]{2,1,0:T(8,128)(2,1)S(1)} async-done(((bf16[128,64,128]{2,1,0:T(8,128)(2,1)}), bf16[128,64,128]{2,1,0:T(8,128)(2,1)S(1)}, u32[]{:S(2)}, u32[]{:S(2)}) %all-to-all-start) | async-done | bytes 2097184 | tf_op jit(solution)/shard_map/all_to_all | solution.py:140
  61.0 2.1 collective-permute-start
  63.0 7.6 %collective-permute-start.1 = (bf16[132,2048]{1,0:T(8,128)(2,1)S(1)}, bf16[132,2048]{1,0:T(8,128)(2,1)S(1)}, u32[]{:S(2)}, u32[]{:S(2)}) collective-permute-start(bf16[132,2048]{1,0:T(8,128)(2,1)S(1)} %constant_dynamic-update-slice_fusion.refs_0_), channel_id=1, source_target_pairs={{2,0},{3,1},{4,2},{5,3},{6,4},{7,5},{8,6},{9,7},{10,8},{11,9},{12,... | collective-permute-start | bytes 1622024 | tf_op jit(solution)/shard_map/ppermute | solution.py:19
  71.5 9.4 %collective-permute-done.refs_1_ = bf16[132,2048]{1,0:T(8,128)(2,1)S(1)} collective-permute-done((bf16[132,2048]{1,0:T(8,128)(2,1)S(1)}, bf16[132,2048]{1,0:T(8,128)(2,1)S(1)}, u32[]{:S(2)}, u32[]{:S(2)}) %collective-permute-start) | collective-permute-done | bytes 540704 | tf_op jit(solution)/shard_map/ppermute | solution.py:19
  80.9 1.9 collective-permute-start.2
  83.7 7.6 %collective-permute-start.3 = (bf16[132,2048]{1,0:T(8,128)(2,1)S(1)}, bf16[132,2048]{1,0:T(8,128)(2,1)S(1)}, u32[]{:S(2)}, u32[]{:S(2)}) collective-permute-start(bf16[132,2048]{1,0:T(8,128)(2,1)S(1)} %collective-permute-done.1.refs_2_), channel_id=1, source_target_pairs={{2,0},{3,1},{4,2},{5,3},{6,4},{7,5},{8,6},{9,7},{10,8},{11,9},{12,... | collective-permute-start | bytes 1622024 | tf_op jit(solution)/shard_map/ppermute | solution.py:19
  92.2 7.7 %collective-permute-done.2.refs_3_ = bf16[132,2048]{1,0:T(8,128)(2,1)S(1)} collective-permute-done((bf16[132,2048]{1,0:T(8,128)(2,1)S(1)}, bf16[132,2048]{1,0:T(8,128)(2,1)S(1)}, u32[]{:S(2)}, u32[]{:S(2)}) %collective-permute-start.2) | collective-permute-done | bytes 540704 | tf_op jit(solution)/shard_map/ppermute | solution.py:19
  99.9 1.9 collective-permute-start.4
  102.7 7.6 %collective-permute-start.5 = (bf16[132,2048]{1,0:T(8,128)(2,1)S(1)}, bf16[132,2048]{1,0:T(8,128)(2,1)S(1)}, u32[]{:S(2)}, u32[]{:S(2)}) collective-permute-start(bf16[132,2048]{1,0:T(8,128)(2,1)S(1)} %collective-permute-done.3.refs_4_), channel_id=1, source_target_pairs={{2,0},{3,1},{4,2},{5,3},{6,4},{7,5},{8,6},{9,7},{10,8},{11,9},{12,... | collective-permute-start | bytes 1622024 | tf_op jit(solution)/shard_map/ppermute | solution.py:19
  111.1 6.8 %collective-permute-done.4.refs_5_ = bf16[132,2048]{1,0:T(8,128)(2,1)S(1)} collective-permute-done((bf16[132,2048]{1,0:T(8,128)(2,1)S(1)}, bf16[132,2048]{1,0:T(8,128)(2,1)S(1)}, u32[]{:S(2)}, u32[]{:S(2)}) %collective-permute-start.4) | collective-permute-done | bytes 540704 | tf_op jit(solution)/shard_map/ppermute | solution.py:19
  117.9 1.9 collective-permute-start.6
  120.8 7.6 %collective-permute-start.7 = (bf16[132,2048]{1,0:T(8,128)(2,1)S(1)}, bf16[132,2048]{1,0:T(8,128)(2,1)S(1)}, u32[]{:S(2)}, u32[]{:S(2)}) collective-permute-start(bf16[132,2048]{1,0:T(8,128)(2,1)S(1)} %collective-permute-done.5.refs_6_), channel_id=1, source_target_pairs={{2,0},{3,1},{4,2},{5,3},{6,4},{7,5},{8,6},{9,7},{10,8},{11,9},{12,... | collective-permute-start | bytes 1622024 | tf_op jit(solution)/shard_map/ppermute | solution.py:19
  129.2 5.9 %collective-permute-done.6.refs_7_ = bf16[132,2048]{1,0:T(8,128)(2,1)S(1)} collective-permute-done((bf16[132,2048]{1,0:T(8,128)(2,1)S(1)}, bf16[132,2048]{1,0:T(8,128)(2,1)S(1)}, u32[]{:S(2)}, u32[]{:S(2)}) %collective-permute-start.6) | collective-permute-done | bytes 540704 | tf_op jit(solution)/shard_map/ppermute | solution.py:19
  137.9 4.2 %collective-permute-start.8 = (bf16[9,132,2048]{2,1,0:T(8,128)(2,1)}, bf16[9,132,2048]{2,1,0:T(8,128)(2,1)}, u32[]{:S(2)}, u32[]{:S(2)}) collective-permute-start(bf16[9,132,2048]{2,1,0:T(8,128)(2,1)} %bitcast_dynamic-update-slice_fusion), channel_id=1, source_target_pairs={{0,1},{1,0},{2,3},{3,2},{4,5},{5,4},{6,7},{7,6},{8,9},{9,8},{10,11... | collective-permute-start | bytes 14598152 | tf_op jit(solution)/shard_map/ppermute | solution.py:167
  144.6 1.4 compare_convert_fusion
  146.0 2.7 %copy.31 = bf16[128,64,128]{2,0,1:T(8,128)(2,1)} copy(bf16[128,64,128]{2,1,0:T(8,128)(2,1)S(1)} %all-to-all-done) | data formatting | bytes 4194304 | tf_op jit(solution)/shard_map/all_to_all | solution.py:140
  156.3 49.8 %shard_map.77 = (bf16[128,8192]{1,0:T(8,128)(2,1)}, f32[8,128,128]{2,1,0:T(8,128)}) custom-call(s32[18]{0:T(128)} %copy-done.10, bf16[64,128,128]{2,1,0:T(8,128)(2,1)} %bitcast.78, bf16[8,128,128]{2,1,0:T(8,128)(2,1)} %pad.6.q0t_ref, bf16[9,132,2048]{2,1,0:T(8,128)(2,1)} %collective-permute-done.8.stack_ref, bf16[132,2048]{1,0:T(8,128)(2,1)} %copy-done.1, ...), custom_call_target="tpu_custom_call" | custom-call | tf_op jit(solution)/shard_map/pallas_call | solution.py:109
  206.2 1.1 fusion
  (77 shorter events, 21.9 us)
Async XLA Ops:
  0.6 206.8 %copy-start = (bf16[8192,16]{0,1:T(8,128)(2,1)S(1)}, bf16[8192,16]{0,1:T(8,128)(2,1)}, u32[]{:S(2)}) copy-start(bf16[8192,16]{0,1:T(8,128)(2,1)} %param.12) | copy-start | bytes 786436
  3.6 22.3 %all-to-all-start.1 = ((bf16[128,16,128]{2,1,0:T(8,128)(2,1)}), bf16[128,16,128]{2,1,0:T(8,128)(2,1)S(1)}, u32[]{:S(2)}, u32[]{:S(2)}) async-start(bf16[128,16,128]{2,1,0:T(8,128)(2,1)} %pad_maximum_fusion), calls=%async_computation.1 | async-start | bytes 1048576 | tf_op jit(solution)/shard_map/all_to_all | solution.py:143
  25.9 35.1 %all-to-all-start = ((bf16[128,64,128]{2,1,0:T(8,128)(2,1)}), bf16[128,64,128]{2,1,0:T(8,128)(2,1)S(1)}, u32[]{:S(2)}, u32[]{:S(2)}) async-start(bf16[128,64,128]{2,1,0:T(8,128)(2,1)} %copy.22), calls=%async_computation | async-start | bytes 4194304 | tf_op jit(solution)/shard_map/all_to_all | solution.py:140
  61.0 77.0 %copy-start.1 = (bf16[132,2048]{1,0:T(8,128)(2,1)}, bf16[132,2048]{1,0:T(8,128)(2,1)S(1)}, u32[]{:S(2)}) copy-start(bf16[132,2048]{1,0:T(8,128)(2,1)S(1)} %constant_dynamic-update-slice_fusion.refs_0_) | copy-start | bytes 1622020
  61.0 81.2 %copy-start.11 = (s32[32]{0:T(128)S(1)}, s32[32]{0:T(128)}, u32[]{:S(2)}) copy-start(s32[32]{0:T(128)} %param.11) | copy-start | bytes 388
  61.0 81.5 %copy-start.12 = (s32[9]{0:T(128)S(1)}, s32[9]{0:T(128)}, u32[]{:S(2)}) copy-start(s32[9]{0:T(128)} %constant.71.clone) | copy-start | bytes 112
  61.0 19.9 %collective-permute-start = (bf16[132,2048]{1,0:T(8,128)(2,1)S(1)}, bf16[132,2048]{1,0:T(8,128)(2,1)S(1)}, u32[]{:S(2)}, u32[]{:S(2)}) collective-permute-start(bf16[132,2048]{1,0:T(8,128)(2,1)S(1)} %constant_dynamic-update-slice_fusion.refs_0_), channel_id=1, source_target_pairs={{0,2},{1,3},{2,4},{3,5},{4,6},{5,7},{6,8},{7,9},{8,10},{9,11},{10,... | collective-permute-start | bytes 1622024 | tf_op jit(solution)/shard_map/ppermute | solution.py:19
  63.0 20.7 %collective-permute-start.1 = (bf16[132,2048]{1,0:T(8,128)(2,1)S(1)}, bf16[132,2048]{1,0:T(8,128)(2,1)S(1)}, u32[]{:S(2)}, u32[]{:S(2)}) collective-permute-start(bf16[132,2048]{1,0:T(8,128)(2,1)S(1)} %constant_dynamic-update-slice_fusion.refs_0_), channel_id=1, source_target_pairs={{2,0},{3,1},{4,2},{5,3},{6,4},{7,5},{8,6},{9,7},{10,8},{11,9},{12,... | collective-permute-start | bytes 1622024 | tf_op jit(solution)/shard_map/ppermute | solution.py:19
  80.9 67.8 %copy-start.2 = (bf16[132,2048]{1,0:T(8,128)(2,1)}, bf16[132,2048]{1,0:T(8,128)(2,1)S(1)}, u32[]{:S(2)}) copy-start(bf16[132,2048]{1,0:T(8,128)(2,1)S(1)} %collective-permute-done.refs_1_) | copy-start | bytes 1622020
  80.9 18.9 %collective-permute-start.2 = (bf16[132,2048]{1,0:T(8,128)(2,1)S(1)}, bf16[132,2048]{1,0:T(8,128)(2,1)S(1)}, u32[]{:S(2)}, u32[]{:S(2)}) collective-permute-start(bf16[132,2048]{1,0:T(8,128)(2,1)S(1)} %collective-permute-done.refs_1_), channel_id=1, source_target_pairs={{0,2},{1,3},{2,4},{3,5},{4,6},{5,7},{6,8},{7,9},{8,10},{9,11},{10,... | collective-permute-start | bytes 1622024 | tf_op jit(solution)/shard_map/ppermute | solution.py:19
  83.7 58.4 %copy-start.3 = (bf16[132,2048]{1,0:T(8,128)(2,1)}, bf16[132,2048]{1,0:T(8,128)(2,1)S(1)}, u32[]{:S(2)}) copy-start(bf16[132,2048]{1,0:T(8,128)(2,1)S(1)} %collective-permute-done.1.refs_2_) | copy-start | bytes 1622020
  83.7 18.9 %collective-permute-start.3 = (bf16[132,2048]{1,0:T(8,128)(2,1)S(1)}, bf16[132,2048]{1,0:T(8,128)(2,1)S(1)}, u32[]{:S(2)}, u32[]{:S(2)}) collective-permute-start(bf16[132,2048]{1,0:T(8,128)(2,1)S(1)} %collective-permute-done.1.refs_2_), channel_id=1, source_target_pairs={{2,0},{3,1},{4,2},{5,3},{6,4},{7,5},{8,6},{9,7},{10,8},{11,9},{12,... | collective-permute-start | bytes 1622024 | tf_op jit(solution)/shard_map/ppermute | solution.py:19
  99.9 42.3 %copy-start.4 = (bf16[132,2048]{1,0:T(8,128)(2,1)}, bf16[132,2048]{1,0:T(8,128)(2,1)S(1)}, u32[]{:S(2)}) copy-start(bf16[132,2048]{1,0:T(8,128)(2,1)S(1)} %collective-permute-done.2.refs_3_) | copy-start | bytes 1622020
  99.9 18.1 %collective-permute-start.4 = (bf16[132,2048]{1,0:T(8,128)(2,1)S(1)}, bf16[132,2048]{1,0:T(8,128)(2,1)S(1)}, u32[]{:S(2)}, u32[]{:S(2)}) collective-permute-start(bf16[132,2048]{1,0:T(8,128)(2,1)S(1)} %collective-permute-done.2.refs_3_), channel_id=1, source_target_pairs={{0,2},{1,3},{2,4},{3,5},{4,6},{5,7},{6,8},{7,9},{8,10},{9,11},{10,... | collective-permute-start | bytes 1622024 | tf_op jit(solution)/shard_map/ppermute | solution.py:19
  102.7 39.5 %copy-start.5 = (bf16[132,2048]{1,0:T(8,128)(2,1)}, bf16[132,2048]{1,0:T(8,128)(2,1)S(1)}, u32[]{:S(2)}) copy-start(bf16[132,2048]{1,0:T(8,128)(2,1)S(1)} %collective-permute-done.3.refs_4_) | copy-start | bytes 1622020
  102.7 18.1 %collective-permute-start.5 = (bf16[132,2048]{1,0:T(8,128)(2,1)S(1)}, bf16[132,2048]{1,0:T(8,128)(2,1)S(1)}, u32[]{:S(2)}, u32[]{:S(2)}) collective-permute-start(bf16[132,2048]{1,0:T(8,128)(2,1)S(1)} %collective-permute-done.3.refs_4_), channel_id=1, source_target_pairs={{2,0},{3,1},{4,2},{5,3},{6,4},{7,5},{8,6},{9,7},{10,8},{11,9},{12,... | collective-permute-start | bytes 1622024 | tf_op jit(solution)/shard_map/ppermute | solution.py:19
  117.9 24.2 %copy-start.6 = (bf16[132,2048]{1,0:T(8,128)(2,1)}, bf16[132,2048]{1,0:T(8,128)(2,1)S(1)}, u32[]{:S(2)}) copy-start(bf16[132,2048]{1,0:T(8,128)(2,1)S(1)} %collective-permute-done.4.refs_5_) | copy-start | bytes 1622020
  117.9 17.2 %collective-permute-start.6 = (bf16[132,2048]{1,0:T(8,128)(2,1)S(1)}, bf16[132,2048]{1,0:T(8,128)(2,1)S(1)}, u32[]{:S(2)}, u32[]{:S(2)}) collective-permute-start(bf16[132,2048]{1,0:T(8,128)(2,1)S(1)} %collective-permute-done.4.refs_5_), channel_id=1, source_target_pairs={{0,2},{1,3},{2,4},{3,5},{4,6},{5,7},{6,8},{7,9},{8,10},{9,11},{10,... | collective-permute-start | bytes 1622024 | tf_op jit(solution)/shard_map/ppermute | solution.py:19
  120.8 21.4 %copy-start.7 = (bf16[132,2048]{1,0:T(8,128)(2,1)}, bf16[132,2048]{1,0:T(8,128)(2,1)S(1)}, u32[]{:S(2)}) copy-start(bf16[132,2048]{1,0:T(8,128)(2,1)S(1)} %collective-permute-done.5.refs_6_) | copy-start | bytes 1622020
  120.8 16.2 %collective-permute-start.7 = (bf16[132,2048]{1,0:T(8,128)(2,1)S(1)}, bf16[132,2048]{1,0:T(8,128)(2,1)S(1)}, u32[]{:S(2)}, u32[]{:S(2)}) collective-permute-start(bf16[132,2048]{1,0:T(8,128)(2,1)S(1)} %collective-permute-done.5.refs_6_), channel_id=1, source_target_pairs={{2,0},{3,1},{4,2},{5,3},{6,4},{7,5},{8,6},{9,7},{10,8},{11,9},{12,... | collective-permute-start | bytes 1622024 | tf_op jit(solution)/shard_map/ppermute | solution.py:19
  135.2 7.0 %copy-start.8 = (bf16[132,2048]{1,0:T(8,128)(2,1)}, bf16[132,2048]{1,0:T(8,128)(2,1)S(1)}, u32[]{:S(2)}) copy-start(bf16[132,2048]{1,0:T(8,128)(2,1)S(1)} %collective-permute-done.6.refs_7_) | copy-start | bytes 1622020
  137.0 5.2 %copy-start.9 = (bf16[132,2048]{1,0:T(8,128)(2,1)}, bf16[132,2048]{1,0:T(8,128)(2,1)S(1)}, u32[]{:S(2)}) copy-start(bf16[132,2048]{1,0:T(8,128)(2,1)S(1)} %collective-permute-done.7.refs_8_) | copy-start | bytes 1622020
  137.9 16.2 %collective-permute-start.8 = (bf16[9,132,2048]{2,1,0:T(8,128)(2,1)}, bf16[9,132,2048]{2,1,0:T(8,128)(2,1)}, u32[]{:S(2)}, u32[]{:S(2)}) collective-permute-start(bf16[9,132,2048]{2,1,0:T(8,128)(2,1)} %bitcast_dynamic-update-slice_fusion), channel_id=1, source_target_pairs={{0,1},{1,0},{2,3},{3,2},{4,5},{5,4},{6,7},{7,6},{8,9},{9,8},{10,11... | collective-permute-start | bytes 14598152 | tf_op jit(solution)/shard_map/ppermute | solution.py:167
  146.0 10.3 %copy-start.10 = (s32[18]{0:T(128)}, s32[18]{0:T(128)S(1)}, u32[]{:S(2)}) copy-start(s32[18]{0:T(128)S(1)} %constant_dynamic-update-slice_fusion.10.flags_ref) | copy-start | bytes 220
where the time goes:
time: 210 us; the launch traced here: 208 us
  waiting for transfers between devices  64.6 us (31%)
  starting transfers between devices  59.5 us (28%)
  Pallas kernels  49.8 us (24%)
  local copies, waits for them, and re-layouts  29.6 us (14%)
  other arithmetic  2.85 us (1%)
    pallas_call x1, Pallas kernels, attend(): pl.pallas_call(attention_kernel, out_shape=(jax.ShapeDtypeStruct((rows, h...  49.8 us
    ppermute x8, starting transfers between devices, shifted(): return lax.ppermute(block, axis, route)  38.1 us
    ppermute x8, waiting for transfers between devices, shifted(): return lax.ppermute(block, axis, route)  30.7 us
    all_to_all x1, waiting for transfers between devices, shards(): lax.all_to_all(queries.reshape(devices, heads, DH), 'seq', split_axis=0,...  28.3 us
    unnamed x47, local copies, waits for them, and re-layouts  18 us
    all_to_all x1, starting transfers between devices, shards(): lax.all_to_all(jnp.concatenate([keys.reshape(devices, heads_kv, DH), valu...  10.6 us
    all_to_all x1, starting transfers between devices, shards(): lax.all_to_all(queries.reshape(devices, heads, DH), 'seq', split_axis=0,...  6.66 us
    all_to_all x1, waiting for transfers between devices, shards(): lax.all_to_all(jnp.concatenate([keys.reshape(devices, heads_kv, DH), valu...  5.66 us
  transfers between devices with their start and end apart: 11, of which 7 were waited for; matrix products, arithmetic and copies ran while one was open for 12% of the time, Pallas kernels for 0%

commit v1 on v0

--- a/solution.py
+++ b/solution.py
@@ -30,24 +30,20 @@
 
 
 def attention_kernel(flags_ref, q_ref, q0t_ref, stack_ref, *refs):
-    own = len(refs) - 9
-    out_ref, out0_ref, qt_ref, m_ref, l_ref, acc_ref, m0_ref, l0_ref, acc0_ref = refs[own:]
-    loaders = [lambda cols, r=r: r[0 : q_ref.shape[1], cols] for r in refs[:own]]
+    own = len(refs) - 8
+    out_ref, out0_ref, m_ref, l_ref, acc_ref, m0_ref, l0_ref, acc0_ref = refs[own:]
+    loaders = [lambda cols, r=r: r[0 : q_ref.shape[2], cols] for r in refs[:own]]
     loaders += [
-        lambda cols, i=i: stack_ref[i, 0 : q_ref.shape[1], cols] for i in range(stack_ref.shape[0])
+        lambda cols, i=i: stack_ref[i, 0 : q_ref.shape[2], cols] for i in range(stack_ref.shape[0])
     ]
     heads = q_ref.shape[0]
-    rows = q_ref.shape[1]
+    rows = q_ref.shape[2]
     width_k = stack_ref.shape[2] // 2
     heads_kv = width_k // DH
     group = heads // heads_kv
     factor = DH ** (-0.5)
 
-    def prep(j, carry):
-        qt_ref[j] = q_ref[j].astype(jnp.float32).T.astype(jnp.bfloat16)
-        return carry
-
-    lax.fori_loop(0, heads, prep, 0)
+    qt_ref = q_ref
 
     def merge(first, ms, ls, accs, j, m1, l1, o1):
         if first:
@@ -103,7 +99,7 @@
 
 
 def attend(flags, q_heads, q0t, partner_stack, pieces):
-    heads, rows, _ = q_heads.shape
+    heads, _, rows = q_heads.shape
     heads_kv = q0t.shape[0]
     width = q0t.shape[2]
     return pl.pallas_call(
@@ -116,7 +112,6 @@
         + [pl.BlockSpec(memory_space=pltpu.VMEM)] * (3 + len(pieces)),
         out_specs=(pl.BlockSpec(memory_space=pltpu.VMEM), pl.BlockSpec(memory_space=pltpu.VMEM)),
         scratch_shapes=[
-            pltpu.VMEM((heads, DH, rows), jnp.bfloat16),
             pltpu.VMEM((heads, 1, rows), jnp.float32),
             pltpu.VMEM((heads, 1, rows), jnp.float32),
             pltpu.VMEM((heads, DH, rows), jnp.float32),
@@ -149,7 +144,7 @@
         concat_axis=0,
         tiled=True,
     )
-    q_heads = arrived_q.transpose(1, 0, 2)
+    q_heads = arrived_q.transpose(1, 2, 0)
     own_q0 = arrived_q[0].reshape(-1, 2 * width_k)
     kv = jnp.concatenate([arrived_kv.reshape(row_count, 2 * width_k), own_q0], axis=0)
     owner_doc, first_block = block_docs(lengths, devices)
@@ -172,11 +167,11 @@
     inside = (blocks >= 0) & (blocks < devices)
     docs = jnp.take(owner_doc, jnp.clip(blocks, 0, devices - 1))
     flags = (inside & (docs == my_doc)).astype(jnp.int32).at[0].set(1)
-    firsts = jnp.concatenate(
-        [jnp.stack([p[row_count:] for p in pieces]), partner_stack[:, row_count:]], axis=0
-    )
-    picked = (blocks == first_block[myself]).astype(firsts.dtype)
-    start_q0 = jnp.sum(firsts * picked[:, None, None], axis=0).astype(firsts.dtype)
+    starts = blocks == first_block[myself]
+    firsts = [p[row_count:] for p in pieces] + [partner_stack[i, row_count:] for i in range(len(pieces))]
+    start_q0 = jnp.zeros_like(firsts[0])
+    for t, first in enumerate(firsts):
+        start_q0 = jnp.where(starts[t], first, start_q0)
     q0t = start_q0.reshape(heads_kv, group, DH).transpose(0, 2, 1)
     q0t = jnp.pad(q0t, ((0, 0), (0, 0), (0, DH - group)))
     attended, start_out = attend(flags, q_heads, q0t, partner_stack, pieces)

time: 210 us -> 209 us (level)
  the two profiles are of different devices: /device:TPU:17 before, /device:TPU:25 now
where the time goes in v1:
time: 209 us; the launch traced here: 206 us
  waiting for transfers between devices  64 us (31%)
  starting transfers between devices  60.4 us (29%)
  Pallas kernels  43.1 us (21%)
  local copies, waits for them, and re-layouts  21.6 us (10%)
  other arithmetic  15 us (7%)
    pallas_call x1, Pallas kernels, attend(): pl.pallas_call(attention_kernel, out_shape=(jax.ShapeDtypeStruct((rows, h...  43.1 us
    ppermute x8, starting transfers between devices, shifted(): return lax.ppermute(block, axis, route)  38.1 us
    all_to_all x1, waiting for transfers between devices, shards(): lax.all_to_all(queries.reshape(devices, heads, DH), 'seq', split_axis=0,...  28.1 us
    ppermute x8, waiting for transfers between devices, shifted(): return lax.ppermute(block, axis, route)  27 us
    unnamed x38, local copies, waits for them, and re-layouts  12.8 us
    select_n x1, other arithmetic, shards(): start_q0 = jnp.where(starts[t], first, start_q0)  12.3 us
    all_to_all x1, starting transfers between devices, shards(): lax.all_to_all(jnp.concatenate([keys.reshape(devices, heads_kv, DH), valu...  10.6 us
    all_to_all x1, waiting for transfers between devices, shards(): lax.all_to_all(jnp.concatenate([keys.reshape(devices, heads_kv, DH), valu...  8.14 us
  transfers between devices with their start and end apart: 11, of which 8 were waited for; matrix products, arithmetic and copies ran while one was open for 9% of the time, Pallas kernels for 0%

profile of v1, /device:TPU:25, one launch (start us, length us, event | category | flops | bytes accessed | tf_op | source)
XLA Modules:
  0.0 205.8 jit_solution(15952035048000714129)
XLA Ops:
  0.6 1.0 copy.25
  3.6 10.6 %all-to-all-start.1 = ((bf16[128,16,128]{2,1,0:T(8,128)(2,1)}), bf16[128,16,128]{2,1,0:T(8,128)(2,1)S(1)}, u32[]{:S(2)}, u32[]{:S(2)}) async-start(bf16[128,16,128]{2,1,0:T(8,128)(2,1)} %pad_maximum_fusion), calls=%async_computation.1 | async-start | bytes 1048576 | tf_op jit(solution)/shard_map/all_to_all | solution.py:138
  14.2 3.5 %copy.23 = bf16[16,8,64,128]{3,2,1,0:T(8,128)(2,1)} copy(bf16[16,8,64,128]{3,1,2,0:T(8,128)(2,1)} %bitcast.116) | data formatting | bytes 4194304
  17.7 8.1 %all-to-all-done.1 = bf16[128,16,128]{2,1,0:T(8,128)(2,1)S(1)} async-done(((bf16[128,16,128]{2,1,0:T(8,128)(2,1)}), bf16[128,16,128]{2,1,0:T(8,128)(2,1)S(1)}, u32[]{:S(2)}, u32[]{:S(2)}) %all-to-all-start.1) | async-done | bytes 524320 | tf_op jit(solution)/shard_map/all_to_all | solution.py:138
  25.8 6.7 %all-to-all-start = ((bf16[128,64,128]{2,1,0:T(8,128)(2,1)}), bf16[128,64,128]{2,1,0:T(8,128)(2,1)S(1)}, u32[]{:S(2)}, u32[]{:S(2)}) async-start(bf16[128,64,128]{2,1,0:T(8,128)(2,1)} %bitcast.114), calls=%async_computation | async-start | bytes 4194304 | tf_op jit(solution)/shard_map/all_to_all | solution.py:135
  32.6 28.1 %all-to-all-done = bf16[128,64,128]{2,1,0:T(8,128)(2,1)S(1)} async-done(((bf16[128,64,128]{2,1,0:T(8,128)(2,1)}), bf16[128,64,128]{2,1,0:T(8,128)(2,1)S(1)}, u32[]{:S(2)}, u32[]{:S(2)}) %all-to-all-start) | async-done | bytes 2097184 | tf_op jit(solution)/shard_map/all_to_all | solution.py:135
  60.8 2.1 collective-permute-start
  62.9 7.6 %collective-permute-start.1 = (bf16[132,2048]{1,0:T(8,128)(2,1)S(1)}, bf16[132,2048]{1,0:T(8,128)(2,1)S(1)}, u32[]{:S(2)}, u32[]{:S(2)}) collective-permute-start(bf16[132,2048]{1,0:T(8,128)(2,1)S(1)} %constant_dynamic-update-slice_fusion.refs_0_), channel_id=1, source_target_pairs={{2,0},{3,1},{4,2},{5,3},{6,4},{7,5},{8,6},{9,7},{10,8},{11,9},{12,... | collective-permute-start | bytes 1622024 | tf_op jit(solution)/shard_map/ppermute | solution.py:19
  71.3 8.5 %collective-permute-done.refs_1_ = bf16[132,2048]{1,0:T(8,128)(2,1)S(1)} collective-permute-done((bf16[132,2048]{1,0:T(8,128)(2,1)S(1)}, bf16[132,2048]{1,0:T(8,128)(2,1)S(1)}, u32[]{:S(2)}, u32[]{:S(2)}) %collective-permute-start) | collective-permute-done | bytes 540704 | tf_op jit(solution)/shard_map/ppermute | solution.py:19
  79.8 1.9 collective-permute-start.2
  82.6 7.6 %collective-permute-start.3 = (bf16[132,2048]{1,0:T(8,128)(2,1)S(1)}, bf16[132,2048]{1,0:T(8,128)(2,1)S(1)}, u32[]{:S(2)}, u32[]{:S(2)}) collective-permute-start(bf16[132,2048]{1,0:T(8,128)(2,1)S(1)} %collective-permute-done.1.refs_2_), channel_id=1, source_target_pairs={{2,0},{3,1},{4,2},{5,3},{6,4},{7,5},{8,6},{9,7},{10,8},{11,9},{12,... | collective-permute-start | bytes 1622024 | tf_op jit(solution)/shard_map/ppermute | solution.py:19
  91.1 6.8 %collective-permute-done.2.refs_3_ = bf16[132,2048]{1,0:T(8,128)(2,1)S(1)} collective-permute-done((bf16[132,2048]{1,0:T(8,128)(2,1)S(1)}, bf16[132,2048]{1,0:T(8,128)(2,1)S(1)}, u32[]{:S(2)}, u32[]{:S(2)}) %collective-permute-start.2) | collective-permute-done | bytes 540704 | tf_op jit(solution)/shard_map/ppermute | solution.py:19
  97.8 1.9 collective-permute-start.4
  100.6 7.6 %collective-permute-start.5 = (bf16[132,2048]{1,0:T(8,128)(2,1)S(1)}, bf16[132,2048]{1,0:T(8,128)(2,1)S(1)}, u32[]{:S(2)}, u32[]{:S(2)}) collective-permute-start(bf16[132,2048]{1,0:T(8,128)(2,1)S(1)} %collective-permute-done.3.refs_4_), channel_id=1, source_target_pairs={{2,0},{3,1},{4,2},{5,3},{6,4},{7,5},{8,6},{9,7},{10,8},{11,9},{12,... | collective-permute-start | bytes 1622024 | tf_op jit(solution)/shard_map/ppermute | solution.py:19
  109.0 5.9 %collective-permute-done.4.refs_5_ = bf16[132,2048]{1,0:T(8,128)(2,1)S(1)} collective-permute-done((bf16[132,2048]{1,0:T(8,128)(2,1)S(1)}, bf16[132,2048]{1,0:T(8,128)(2,1)S(1)}, u32[]{:S(2)}, u32[]{:S(2)}) %collective-permute-start.4) | collective-permute-done | bytes 540704 | tf_op jit(solution)/shard_map/ppermute | solution.py:19
  115.0 1.9 collective-permute-start.6
  117.8 7.6 %collective-permute-start.7 = (bf16[132,2048]{1,0:T(8,128)(2,1)S(1)}, bf16[132,2048]{1,0:T(8,128)(2,1)S(1)}, u32[]{:S(2)}, u32[]{:S(2)}) collective-permute-start(bf16[132,2048]{1,0:T(8,128)(2,1)S(1)} %collective-permute-done.5.refs_6_), channel_id=1, source_target_pairs={{2,0},{3,1},{4,2},{5,3},{6,4},{7,5},{8,6},{9,7},{10,8},{11,9},{12,... | collective-permute-start | bytes 1622024 | tf_op jit(solution)/shard_map/ppermute | solution.py:19
  126.3 5.0 %collective-permute-done.6.refs_7_ = bf16[132,2048]{1,0:T(8,128)(2,1)S(1)} collective-permute-done((bf16[132,2048]{1,0:T(8,128)(2,1)S(1)}, bf16[132,2048]{1,0:T(8,128)(2,1)S(1)}, u32[]{:S(2)}, u32[]{:S(2)}) %collective-permute-start.6) | collective-permute-done | bytes 540704 | tf_op jit(solution)/shard_map/ppermute | solution.py:19
  134.0 5.1 %collective-permute-start.8 = (bf16[9,132,2048]{2,1,0:T(8,128)(2,1)}, bf16[9,132,2048]{2,1,0:T(8,128)(2,1)}, u32[]{:S(2)}, u32[]{:S(2)}) collective-permute-start(bf16[9,132,2048]{2,1,0:T(8,128)(2,1)} %bitcast_dynamic-update-slice_fusion), channel_id=1, source_target_pairs={{0,1},{1,0},{2,3},{3,2},{4,5},{5,4},{6,7},{7,6},{8,9},{9,8},{10,11... | collective-permute-start | bytes 14598152 | tf_op jit(solution)/shard_map/ppermute | solution.py:162
  141.6 1.4 broadcast_compare_fusion
  143.8 2.9 %copy.20 = bf16[128,64,128]{0,2,1:T(8,128)(2,1)} copy(bf16[128,64,128]{2,1,0:T(8,128)(2,1)S(1)} %all-to-all-done) | data formatting | bytes 4194304 | tf_op jit(solution)/shard_map/all_to_all | solution.py:135
  147.4 12.3 %fusion.15 = bf16[4,2048]{1,0:T(4,128)(2,1)S(1)} fusion(bf16[9,132,2048]{2,1,0:T(8,128)(2,1)} %collective-permute-done.8.stack_ref, pred[]{:T(512)} %bitcast.24, pred[]{:T(512)} %bitcast.22, pred[]{:T(512)} %bitcast.20, pred[]{:T(512)} %bitcast.18, pred[]{:T(512)} %bitcast.7, bf16[4,2048]{1,0:T(4,128)(2,1)S(1)} %reshape_squeeze.3, pred[]{:T(512)} %bitcast.42, ...), kind=kLoop, calls=%fused_computation.36 | loop fusion | flops 147456 | bytes 311314 | tf_op jit(solution)/shard_map/jit(_where)/select_n | solution.py:174
  160.7 43.1 %shard_map.77 = (bf16[128,8192]{1,0:T(8,128)(2,1)}, f32[8,128,128]{2,1,0:T(8,128)}) custom-call(s32[18]{0:T(128)} %copy-done.10, bf16[64,128,128]{2,1,0:T(8,128)(2,1)} %bitcast.115, bf16[8,128,128]{2,1,0:T(8,128)(2,1)} %pad.6.q0t_ref, bf16[9,132,2048]{2,1,0:T(8,128)(2,1)} %collective-permute-done.8.stack_ref, bf16[132,2048]{1,0:T(8,128)(2,1)} %copy-done.1, ...), custom_call_target="tpu_custom_call" | custom-call | tf_op jit(solution)/shard_map/pallas_call | solution.py:105
  203.8 1.1 fusion
  (66 shorter events, 16.7 us)
Async XLA Ops:
  0.6 204.4 %copy-start = (bf16[8192,16]{0,1:T(8,128)(2,1)S(1)}, bf16[8192,16]{0,1:T(8,128)(2,1)}, u32[]{:S(2)}) copy-start(bf16[8192,16]{0,1:T(8,128)(2,1)} %param.12) | copy-start | bytes 786436
  3.6 22.2 %all-to-all-start.1 = ((bf16[128,16,128]{2,1,0:T(8,128)(2,1)}), bf16[128,16,128]{2,1,0:T(8,128)(2,1)S(1)}, u32[]{:S(2)}, u32[]{:S(2)}) async-start(bf16[128,16,128]{2,1,0:T(8,128)(2,1)} %pad_maximum_fusion), calls=%async_computation.1 | async-start | bytes 1048576 | tf_op jit(solution)/shard_map/all_to_all | solution.py:138
  25.8 34.9 %all-to-all-start = ((bf16[128,64,128]{2,1,0:T(8,128)(2,1)}), bf16[128,64,128]{2,1,0:T(8,128)(2,1)S(1)}, u32[]{:S(2)}, u32[]{:S(2)}) async-start(bf16[128,64,128]{2,1,0:T(8,128)(2,1)} %bitcast.114), calls=%async_computation | async-start | bytes 4194304 | tf_op jit(solution)/shard_map/all_to_all | solution.py:135
  60.8 73.2 %copy-start.1 = (bf16[132,2048]{1,0:T(8,128)(2,1)}, bf16[132,2048]{1,0:T(8,128)(2,1)S(1)}, u32[]{:S(2)}) copy-start(bf16[132,2048]{1,0:T(8,128)(2,1)S(1)} %constant_dynamic-update-slice_fusion.refs_0_) | copy-start | bytes 1622020
  60.8 78.4 %copy-start.11 = (s32[32]{0:T(128)S(1)}, s32[32]{0:T(128)}, u32[]{:S(2)}) copy-start(s32[32]{0:T(128)} %param.11) | copy-start | bytes 388
  60.8 80.0 %copy-start.12 = (s32[9]{0:T(128)S(1)}, s32[9]{0:T(128)}, u32[]{:S(2)}) copy-start(s32[9]{0:T(128)} %constant.70.clone) | copy-start | bytes 112
  60.8 19.0 %collective-permute-start = (bf16[132,2048]{1,0:T(8,128)(2,1)S(1)}, bf16[132,2048]{1,0:T(8,128)(2,1)S(1)}, u32[]{:S(2)}, u32[]{:S(2)}) collective-permute-start(bf16[132,2048]{1,0:T(8,128)(2,1)S(1)} %constant_dynamic-update-slice_fusion.refs_0_), channel_id=1, source_target_pairs={{0,2},{1,3},{2,4},{3,5},{4,6},{5,7},{6,8},{7,9},{8,10},{9,11},{10,... | collective-permute-start | bytes 1622024 | tf_op jit(solution)/shard_map/ppermute | solution.py:19
  62.9 19.7 %collective-permute-start.1 = (bf16[132,2048]{1,0:T(8,128)(2,1)S(1)}, bf16[132,2048]{1,0:T(8,128)(2,1)S(1)}, u32[]{:S(2)}, u32[]{:S(2)}) collective-permute-start(bf16[132,2048]{1,0:T(8,128)(2,1)S(1)} %constant_dynamic-update-slice_fusion.refs_0_), channel_id=1, source_target_pairs={{2,0},{3,1},{4,2},{5,3},{6,4},{7,5},{8,6},{9,7},{10,8},{11,9},{12,... | collective-permute-start | bytes 1622024 | tf_op jit(solution)/shard_map/ppermute | solution.py:19
  79.8 67.6 %copy-start.2 = (bf16[132,2048]{1,0:T(8,128)(2,1)}, bf16[132,2048]{1,0:T(8,128)(2,1)S(1)}, u32[]{:S(2)}) copy-start(bf16[132,2048]{1,0:T(8,128)(2,1)S(1)} %collective-permute-done.refs_1_) | copy-start | bytes 1622020
  79.8 18.0 %collective-permute-start.2 = (bf16[132,2048]{1,0:T(8,128)(2,1)S(1)}, bf16[132,2048]{1,0:T(8,128)(2,1)S(1)}, u32[]{:S(2)}, u32[]{:S(2)}) collective-permute-start(bf16[132,2048]{1,0:T(8,128)(2,1)S(1)} %collective-permute-done.refs_1_), channel_id=1, source_target_pairs={{0,2},{1,3},{2,4},{3,5},{4,6},{5,7},{6,8},{7,9},{8,10},{9,11},{10,... | collective-permute-start | bytes 1622024 | tf_op jit(solution)/shard_map/ppermute | solution.py:19
  82.6 56.5 %copy-start.3 = (bf16[132,2048]{1,0:T(8,128)(2,1)}, bf16[132,2048]{1,0:T(8,128)(2,1)S(1)}, u32[]{:S(2)}) copy-start(bf16[132,2048]{1,0:T(8,128)(2,1)S(1)} %collective-permute-done.1.refs_2_) | copy-start | bytes 1622020
  82.6 18.0 %collective-permute-start.3 = (bf16[132,2048]{1,0:T(8,128)(2,1)S(1)}, bf16[132,2048]{1,0:T(8,128)(2,1)S(1)}, u32[]{:S(2)}, u32[]{:S(2)}) collective-permute-start(bf16[132,2048]{1,0:T(8,128)(2,1)S(1)} %collective-permute-done.1.refs_2_), channel_id=1, source_target_pairs={{2,0},{3,1},{4,2},{5,3},{6,4},{7,5},{8,6},{9,7},{10,8},{11,9},{12,... | collective-permute-start | bytes 1622024 | tf_op jit(solution)/shard_map/ppermute | solution.py:19
  97.8 41.3 %copy-start.4 = (bf16[132,2048]{1,0:T(8,128)(2,1)}, bf16[132,2048]{1,0:T(8,128)(2,1)S(1)}, u32[]{:S(2)}) copy-start(bf16[132,2048]{1,0:T(8,128)(2,1)S(1)} %collective-permute-done.2.refs_3_) | copy-start | bytes 1622020
  97.8 17.1 %collective-permute-start.4 = (bf16[132,2048]{1,0:T(8,128)(2,1)S(1)}, bf16[132,2048]{1,0:T(8,128)(2,1)S(1)}, u32[]{:S(2)}, u32[]{:S(2)}) collective-permute-start(bf16[132,2048]{1,0:T(8,128)(2,1)S(1)} %collective-permute-done.2.refs_3_), channel_id=1, source_target_pairs={{0,2},{1,3},{2,4},{3,5},{4,6},{5,7},{6,8},{7,9},{8,10},{9,11},{10,... | collective-permute-start | bytes 1622024 | tf_op jit(solution)/shard_map/ppermute | solution.py:19
  100.6 38.6 %copy-start.5 = (bf16[132,2048]{1,0:T(8,128)(2,1)}, bf16[132,2048]{1,0:T(8,128)(2,1)S(1)}, u32[]{:S(2)}) copy-start(bf16[132,2048]{1,0:T(8,128)(2,1)S(1)} %collective-permute-done.3.refs_4_) | copy-start | bytes 1622020
  100.6 17.2 %collective-permute-start.5 = (bf16[132,2048]{1,0:T(8,128)(2,1)S(1)}, bf16[132,2048]{1,0:T(8,128)(2,1)S(1)}, u32[]{:S(2)}, u32[]{:S(2)}) collective-permute-start(bf16[132,2048]{1,0:T(8,128)(2,1)S(1)} %collective-permute-done.3.refs_4_), channel_id=1, source_target_pairs={{2,0},{3,1},{4,2},{5,3},{6,4},{7,5},{8,6},{9,7},{10,8},{11,9},{12,... | collective-permute-start | bytes 1622024 | tf_op jit(solution)/shard_map/ppermute | solution.py:19
  115.0 24.2 %copy-start.6 = (bf16[132,2048]{1,0:T(8,128)(2,1)}, bf16[132,2048]{1,0:T(8,128)(2,1)S(1)}, u32[]{:S(2)}) copy-start(bf16[132,2048]{1,0:T(8,128)(2,1)S(1)} %collective-permute-done.4.refs_5_) | copy-start | bytes 1622020
  115.0 16.3 %collective-permute-start.6 = (bf16[132,2048]{1,0:T(8,128)(2,1)S(1)}, bf16[132,2048]{1,0:T(8,128)(2,1)S(1)}, u32[]{:S(2)}, u32[]{:S(2)}) collective-permute-start(bf16[132,2048]{1,0:T(8,128)(2,1)S(1)} %collective-permute-done.4.refs_5_), channel_id=1, source_target_pairs={{0,2},{1,3},{2,4},{3,5},{4,6},{5,7},{6,8},{7,9},{8,10},{9,11},{10,... | collective-permute-start | bytes 1622024 | tf_op jit(solution)/shard_map/ppermute | solution.py:19
  117.8 21.4 %copy-start.7 = (bf16[132,2048]{1,0:T(8,128)(2,1)}, bf16[132,2048]{1,0:T(8,128)(2,1)S(1)}, u32[]{:S(2)}) copy-start(bf16[132,2048]{1,0:T(8,128)(2,1)S(1)} %collective-permute-done.5.refs_6_) | copy-start | bytes 1622020
  117.8 15.3 %collective-permute-start.7 = (bf16[132,2048]{1,0:T(8,128)(2,1)S(1)}, bf16[132,2048]{1,0:T(8,128)(2,1)S(1)}, u32[]{:S(2)}, u32[]{:S(2)}) collective-permute-start(bf16[132,2048]{1,0:T(8,128)(2,1)S(1)} %collective-permute-done.5.refs_6_), channel_id=1, source_target_pairs={{2,0},{3,1},{4,2},{5,3},{6,4},{7,5},{8,6},{9,7},{10,8},{11,9},{12,... | collective-permute-start | bytes 1622024 | tf_op jit(solution)/shard_map/ppermute | solution.py:19
  131.3 7.9 %copy-start.8 = (bf16[132,2048]{1,0:T(8,128)(2,1)}, bf16[132,2048]{1,0:T(8,128)(2,1)S(1)}, u32[]{:S(2)}) copy-start(bf16[132,2048]{1,0:T(8,128)(2,1)S(1)} %collective-permute-done.6.refs_7_) | copy-start | bytes 1622020
  133.1 6.1 %copy-start.9 = (bf16[132,2048]{1,0:T(8,128)(2,1)}, bf16[132,2048]{1,0:T(8,128)(2,1)S(1)}, u32[]{:S(2)}) copy-start(bf16[132,2048]{1,0:T(8,128)(2,1)S(1)} %collective-permute-done.7.refs_8_) | copy-start | bytes 1622020
  134.0 13.4 %collective-permute-start.8 = (bf16[9,132,2048]{2,1,0:T(8,128)(2,1)}, bf16[9,132,2048]{2,1,0:T(8,128)(2,1)}, u32[]{:S(2)}, u32[]{:S(2)}) collective-permute-start(bf16[9,132,2048]{2,1,0:T(8,128)(2,1)} %bitcast_dynamic-update-slice_fusion), channel_id=1, source_target_pairs={{0,1},{1,0},{2,3},{3,2},{4,5},{5,4},{6,7},{7,6},{8,9},{9,8},{10,11... | collective-permute-start | bytes 14598152 | tf_op jit(solution)/shard_map/ppermute | solution.py:162
  143.0 17.7 %copy-start.10 = (s32[18]{0:T(128)}, s32[18]{0:T(128)S(1)}, u32[]{:S(2)}) copy-start(s32[18]{0:T(128)S(1)} %constant_dynamic-update-slice_fusion.1.flags_ref) | copy-start | bytes 220

commit v2 on v1

--- a/solution.py
+++ b/solution.py
@@ -29,35 +29,28 @@
     return (owner_doc, first_block)
 
 
-def attention_kernel(flags_ref, q_ref, q0t_ref, stack_ref, *refs):
+def attention_kernel(meta_ref, q_ref, stack_ref, *refs):
     own = len(refs) - 8
     out_ref, out0_ref, m_ref, l_ref, acc_ref, m0_ref, l0_ref, acc0_ref = refs[own:]
-    loaders = [lambda cols, r=r: r[0 : q_ref.shape[2], cols] for r in refs[:own]]
-    loaders += [
-        lambda cols, i=i: stack_ref[i, 0 : q_ref.shape[2], cols] for i in range(stack_ref.shape[0])
-    ]
+    rows = q_ref.shape[2]
+    loaders = [lambda cols, r=r: r[:, cols] for r in refs[:own]]
+    loaders += [lambda cols, i=i: stack_ref[i, :, cols] for i in range(stack_ref.shape[0])]
+    tiles = len(loaders)
     heads = q_ref.shape[0]
-    rows = q_ref.shape[2]
-    width_k = stack_ref.shape[2] // 2
+    width_k = (stack_ref.shape[2] - DH) // 2
     heads_kv = width_k // DH
     group = heads // heads_kv
     factor = DH ** (-0.5)
+    q0s_ref = out0_ref
 
-    qt_ref = q_ref
+    for t in range(tiles):
 
-    def merge(first, ms, ls, accs, j, m1, l1, o1):
-        if first:
-            ms[j] = m1
-            ls[j] = l1
-            accs[j] = o1
-        else:
-            m0 = ms[j]
-            mn = jnp.maximum(m0, m1)
-            a = jnp.exp(m0 - mn)
-            b = jnp.exp(m1 - mn)
-            ms[j] = mn
-            ls[j] = ls[j] * a + l1 * b
-            accs[j] = accs[j] * a + o1 * b
+        @pl.when(meta_ref[tiles] == t)
+        def _(load=loaders[t]):
+            q0s_ref[...] = load(pl.ds(2 * width_k, DH)).astype(jnp.float32)
+
+    q0t = q0s_ref[...].astype(jnp.bfloat16)
+    column_head = lax.broadcasted_iota(jnp.int32, (1, DH), 1) // group
 
     def scored(k, vt, qt):
         st = jnp.dot(k, qt, preferred_element_type=jnp.float32) * factor
@@ -67,6 +60,26 @@
         ot = jnp.dot(vt, p.astype(jnp.bfloat16), preferred_element_type=jnp.float32)
         return m1, l1, ot
 
+    def merge(first, ms, ls, accs, j, m1, l1, o1, mask=None):
+        def put(ref, value):
+            if mask is None:
+                ref[j] = value
+            else:
+                ref[j] = jnp.where(mask, value, ref[j])
+
+        if first:
+            put(ms, m1)
+            put(ls, l1)
+            put(accs, o1)
+        else:
+            m0 = ms[j]
+            mn = jnp.maximum(m0, m1)
+            a = jnp.exp(m0 - mn)
+            b = jnp.exp(m1 - mn)
+            put(ms, mn)
+            put(ls, ls[j] * a + l1 * b)
+            put(accs, accs[j] * a + o1 * b)
+
     def tile_step(load, first):
         def one_head(h, carry):
             kcol = pl.multiple_of(h * DH, DH)
@@ -75,16 +88,16 @@
             vt = load(pl.ds(vcol, DH)).astype(jnp.float32).T.astype(jnp.bfloat16)
             for g in range(group):
                 j = h * group + g
-                merge(first, m_ref, l_ref, acc_ref, j, *scored(k, vt, qt_ref[j]))
-            merge(first, m0_ref, l0_ref, acc0_ref, h, *scored(k, vt, q0t_ref[h]))
+                merge(first, m_ref, l_ref, acc_ref, j, *scored(k, vt, q_ref[j]))
+            merge(first, m0_ref, l0_ref, acc0_ref, 0, *scored(k, vt, q0t), mask=column_head == h)
             return carry
 
         lax.fori_loop(0, heads_kv, one_head, 0)
 
     tile_step(loaders[0], True)
-    for t in range(1, len(loaders)):
+    for t in range(1, tiles):
 
-        @pl.when(flags_ref[t] > 0)
+        @pl.when(meta_ref[t] > 0)
         def _(load=loaders[t]):
             tile_step(load, False)
 
@@ -94,33 +107,30 @@
         return carry
 
     lax.fori_loop(0, heads, finish, 0)
-    for h in range(heads_kv):
-        out0_ref[h] = acc0_ref[h] / l0_ref[h]
+    out0_ref[...] = acc0_ref[0] / l0_ref[0]
 
 
-def attend(flags, q_heads, q0t, partner_stack, pieces):
+def attend(meta, q_heads, partner_stack, pieces):
     heads, _, rows = q_heads.shape
-    heads_kv = q0t.shape[0]
-    width = q0t.shape[2]
     return pl.pallas_call(
         attention_kernel,
         out_shape=(
             jax.ShapeDtypeStruct((rows, heads * DH), jnp.bfloat16),
-            jax.ShapeDtypeStruct((heads_kv, DH, width), jnp.float32),
+            jax.ShapeDtypeStruct((DH, DH), jnp.float32),
         ),
         in_specs=[pl.BlockSpec(memory_space=pltpu.SMEM)]
-        + [pl.BlockSpec(memory_space=pltpu.VMEM)] * (3 + len(pieces)),
+        + [pl.BlockSpec(memory_space=pltpu.VMEM)] * (2 + len(pieces)),
         out_specs=(pl.BlockSpec(memory_space=pltpu.VMEM), pl.BlockSpec(memory_space=pltpu.VMEM)),
         scratch_shapes=[
             pltpu.VMEM((heads, 1, rows), jnp.float32),
             pltpu.VMEM((heads, 1, rows), jnp.float32),
             pltpu.VMEM((heads, DH, rows), jnp.float32),
-            pltpu.VMEM((heads_kv, 1, width), jnp.float32),
-            pltpu.VMEM((heads_kv, 1, width), jnp.float32),
-            pltpu.VMEM((heads_kv, DH, width), jnp.float32),
+            pltpu.VMEM((1, 1, DH), jnp.float32),
+            pltpu.VMEM((1, 1, DH), jnp.float32),
+            pltpu.VMEM((1, DH, DH), jnp.float32),
         ],
         compiler_params=pltpu.CompilerParams(vmem_limit_bytes=56 * 1024 * 1024),
-    )(flags, q_heads, q0t, partner_stack, *pieces)
+    )(meta, q_heads, partner_stack, *pieces)
 
 
 def shards(queries, keys, values, lengths, class_weight):
@@ -145,8 +155,8 @@
         tiled=True,
     )
     q_heads = arrived_q.transpose(1, 2, 0)
-    own_q0 = arrived_q[0].reshape(-1, 2 * width_k)
-    kv = jnp.concatenate([arrived_kv.reshape(row_count, 2 * width_k), own_q0], axis=0)
+    own_q0t = jnp.pad(arrived_q[0].T, ((0, 0), (0, DH - heads)))
+    kv = jnp.concatenate([arrived_kv.reshape(row_count, 2 * width_k), own_q0t], axis=1)
     owner_doc, first_block = block_docs(lengths, devices)
     my_doc = owner_doc[myself]
     partner = myself + 1 - 2 * (myself % 2)
@@ -167,15 +177,10 @@
     inside = (blocks >= 0) & (blocks < devices)
     docs = jnp.take(owner_doc, jnp.clip(blocks, 0, devices - 1))
     flags = (inside & (docs == my_doc)).astype(jnp.int32).at[0].set(1)
-    starts = blocks == first_block[myself]
-    firsts = [p[row_count:] for p in pieces] + [partner_stack[i, row_count:] for i in range(len(pieces))]
-    start_q0 = jnp.zeros_like(firsts[0])
-    for t, first in enumerate(firsts):
-        start_q0 = jnp.where(starts[t], first, start_q0)
-    q0t = start_q0.reshape(heads_kv, group, DH).transpose(0, 2, 1)
-    q0t = jnp.pad(q0t, ((0, 0), (0, 0), (0, DH - group)))
-    attended, start_out = attend(flags, q_heads, q0t, partner_stack, pieces)
-    start_row = start_out[:, :, :group].transpose(0, 2, 1).reshape(1, width_q).astype(jnp.bfloat16)
+    pick = jnp.argmax(blocks == first_block[myself]).astype(jnp.int32)
+    meta = jnp.concatenate([flags, pick[None]])
+    attended, start_out = attend(meta, q_heads, partner_stack, pieces)
+    start_row = start_out[:, :heads].T.reshape(1, width_q).astype(jnp.bfloat16)
     doc_logits = jnp.dot(start_row, class_weight, preferred_element_type=jnp.float32)
     return (attended, doc_logits)
 

time: 209 us -> 194 us (0.928)
  the two profiles are of different devices: /device:TPU:25 before, /device:TPU:7 now
where the time goes in v2:
time: 194 us; the launch traced here: 191 us
  waiting for transfers between devices  68.6 us (35%)
  starting transfers between devices  50.6 us (26%)
  Pallas kernels  43.1 us (22%)
  local copies, waits for them, and re-layouts  21.3 us (11%)
  other arithmetic  5.56 us (3%)
    pallas_call x1, Pallas kernels, attend(): pl.pallas_call(attention_kernel, out_shape=(jax.ShapeDtypeStruct((rows, h...  43.1 us
    ppermute x8, waiting for transfers between devices, shifted(): return lax.ppermute(block, axis, route)  34.2 us
    ppermute x8, starting transfers between devices, shifted(): return lax.ppermute(block, axis, route)  29.8 us
    all_to_all x1, waiting for transfers between devices, shards(): lax.all_to_all(queries.reshape(devices, heads, DH), 'seq', split_axis=0,...  28.4 us
    unnamed x36, local copies, waits for them, and re-layouts  11.7 us
    all_to_all x1, starting transfers between devices, shards(): lax.all_to_all(jnp.concatenate([keys.reshape(devices, heads_kv, DH), valu...  10.8 us
    all_to_all x1, starting transfers between devices, shards(): lax.all_to_all(queries.reshape(devices, heads, DH), 'seq', split_axis=0,...  6.26 us
    all_to_all x1, waiting for transfers between devices, shards(): lax.all_to_all(jnp.concatenate([keys.reshape(devices, heads_kv, DH), valu...  5.99 us
  transfers between devices with their start and end apart: 11, of which 6 were waited for; matrix products, arithmetic and copies ran while one was open for 11% of the time, Pallas kernels for 0%

profile of v2, /device:TPU:7, one launch (start us, length us, event | category | flops | bytes accessed | tf_op | source)
XLA Modules:
  0.0 190.8 jit_solution(11553441926161738383)
XLA Ops:
  0.6 1.0 copy.28
  3.6 10.8 %all-to-all-start.1 = ((bf16[128,16,128]{2,1,0:T(8,128)(2,1)}), bf16[128,16,128]{2,1,0:T(8,128)(2,1)S(1)}, u32[]{:S(2)}, u32[]{:S(2)}) async-start(bf16[128,16,128]{2,1,0:T(8,128)(2,1)} %pad_maximum_fusion), calls=%async_computation.1 | async-start | bytes 1048576 | tf_op jit(solution)/shard_map/all_to_all | solution.py:148
  14.3 3.2 %copy.22 = bf16[128,8192]{0,1:T(8,128)(2,1)S(1)} copy(bf16[128,8192]{1,0:T(8,128)(2,1)} %param.8) | data formatting | bytes 4194304 | tf_op args[0]
  17.6 2.8 %copy.23 = bf16[128,64,128]{2,1,0:T(8,128)(2,1)} copy(bf16[128,64,128]{0,2,1:T(8,128)(2,1)S(1)} %bitcast.47) | data formatting | bytes 4194304 | tf_op jit(solution)/shard_map/reshape | solution.py:146
  20.3 6.0 %all-to-all-done.1 = bf16[128,16,128]{2,1,0:T(8,128)(2,1)S(1)} async-done(((bf16[128,16,128]{2,1,0:T(8,128)(2,1)}), bf16[128,16,128]{2,1,0:T(8,128)(2,1)S(1)}, u32[]{:S(2)}, u32[]{:S(2)}) %all-to-all-start.1) | async-done | bytes 524320 | tf_op jit(solution)/shard_map/all_to_all | solution.py:148
  26.3 6.3 %all-to-all-start = ((bf16[128,64,128]{2,1,0:T(8,128)(2,1)}), bf16[128,64,128]{2,1,0:T(8,128)(2,1)S(1)}, u32[]{:S(2)}, u32[]{:S(2)}) async-start(bf16[128,64,128]{2,1,0:T(8,128)(2,1)} %copy.23), calls=%async_computation | async-start | bytes 4194304 | tf_op jit(solution)/shard_map/all_to_all | solution.py:145
  32.7 28.4 %all-to-all-done = bf16[128,64,128]{2,1,0:T(8,128)(2,1)S(1)} async-done(((bf16[128,64,128]{2,1,0:T(8,128)(2,1)}), bf16[128,64,128]{2,1,0:T(8,128)(2,1)S(1)}, u32[]{:S(2)}, u32[]{:S(2)}) %all-to-all-start) | async-done | bytes 2097184 | tf_op jit(solution)/shard_map/all_to_all | solution.py:145
  61.4 3.1 %collective-permute-start.1 = (bf16[128,2176]{1,0:T(8,128)(2,1)S(1)}, bf16[128,2176]{1,0:T(8,128)(2,1)S(1)}, u32[]{:S(2)}, u32[]{:S(2)}) collective-permute-start(bf16[128,2176]{1,0:T(8,128)(2,1)S(1)} %fusion.1.refs_0_), channel_id=1, source_target_pairs={{2,0},{3,1},{4,2},{5,3},{6,4},{7,5},{8,6},{9,7},{10,8},{11,9},{12,... | collective-permute-start | bytes 1671176 | tf_op jit(solution)/shard_map/ppermute | solution.py:19
  64.5 2.3 %collective-permute-start = (bf16[128,2176]{1,0:T(8,128)(2,1)S(1)}, bf16[128,2176]{1,0:T(8,128)(2,1)S(1)}, u32[]{:S(2)}, u32[]{:S(2)}) collective-permute-start(bf16[128,2176]{1,0:T(8,128)(2,1)S(1)} %fusion.1.refs_0_), channel_id=1, source_target_pairs={{0,2},{1,3},{2,4},{3,5},{4,6},{5,7},{6,8},{7,9},{8,10},{9,11},{10,... | collective-permute-start | bytes 1671176 | tf_op jit(solution)/shard_map/ppermute | solution.py:19
  67.7 8.7 %collective-permute-done.1.refs_2_ = bf16[128,2176]{1,0:T(8,128)(2,1)S(1)} collective-permute-done((bf16[128,2176]{1,0:T(8,128)(2,1)S(1)}, bf16[128,2176]{1,0:T(8,128)(2,1)S(1)}, u32[]{:S(2)}, u32[]{:S(2)}) %collective-permute-start.1) | collective-permute-done | bytes 557088 | tf_op jit(solution)/shard_map/ppermute | solution.py:19
  76.4 6.2 %collective-permute-start.3 = (bf16[128,2176]{1,0:T(8,128)(2,1)S(1)}, bf16[128,2176]{1,0:T(8,128)(2,1)S(1)}, u32[]{:S(2)}, u32[]{:S(2)}) collective-permute-start(bf16[128,2176]{1,0:T(8,128)(2,1)S(1)} %collective-permute-done.1.refs_2_), channel_id=1, source_target_pairs={{2,0},{3,1},{4,2},{5,3},{6,4},{7,5},{8,6},{9,7},{10,8},{11,9},{12,... | collective-permute-start | bytes 1671176 | tf_op jit(solution)/shard_map/ppermute | solution.py:19
  82.6 1.9 %collective-permute-start.2 = (bf16[128,2176]{1,0:T(8,128)(2,1)S(1)}, bf16[128,2176]{1,0:T(8,128)(2,1)S(1)}, u32[]{:S(2)}, u32[]{:S(2)}) collective-permute-start(bf16[128,2176]{1,0:T(8,128)(2,1)S(1)} %collective-permute-done.refs_1_), channel_id=1, source_target_pairs={{0,2},{1,3},{2,4},{3,5},{4,6},{5,7},{6,8},{7,9},{8,10},{9,11},{10,... | collective-permute-start | bytes 1671176 | tf_op jit(solution)/shard_map/ppermute | solution.py:19
  86.3 7.4 %collective-permute-done.3.refs_4_ = bf16[128,2176]{1,0:T(8,128)(2,1)S(1)} collective-permute-done((bf16[128,2176]{1,0:T(8,128)(2,1)S(1)}, bf16[128,2176]{1,0:T(8,128)(2,1)S(1)}, u32[]{:S(2)}, u32[]{:S(2)}) %collective-permute-start.3) | collective-permute-done | bytes 557088 | tf_op jit(solution)/shard_map/ppermute | solution.py:19
  93.6 6.2 %collective-permute-start.5 = (bf16[128,2176]{1,0:T(8,128)(2,1)S(1)}, bf16[128,2176]{1,0:T(8,128)(2,1)S(1)}, u32[]{:S(2)}, u32[]{:S(2)}) collective-permute-start(bf16[128,2176]{1,0:T(8,128)(2,1)S(1)} %collective-permute-done.3.refs_4_), channel_id=1, source_target_pairs={{2,0},{3,1},{4,2},{5,3},{6,4},{7,5},{8,6},{9,7},{10,8},{11,9},{12,... | collective-permute-start | bytes 1671176 | tf_op jit(solution)/shard_map/ppermute | solution.py:19
  99.9 1.9 %collective-permute-start.4 = (bf16[128,2176]{1,0:T(8,128)(2,1)S(1)}, bf16[128,2176]{1,0:T(8,128)(2,1)S(1)}, u32[]{:S(2)}, u32[]{:S(2)}) collective-permute-start(bf16[128,2176]{1,0:T(8,128)(2,1)S(1)} %collective-permute-done.2.refs_3_), channel_id=1, source_target_pairs={{0,2},{1,3},{2,4},{3,5},{4,6},{5,7},{6,8},{7,9},{8,10},{9,11},{10,... | collective-permute-start | bytes 1671176 | tf_op jit(solution)/shard_map/ppermute | solution.py:19
  103.5 6.5 %collective-permute-done.5.refs_6_ = bf16[128,2176]{1,0:T(8,128)(2,1)S(1)} collective-permute-done((bf16[128,2176]{1,0:T(8,128)(2,1)S(1)}, bf16[128,2176]{1,0:T(8,128)(2,1)S(1)}, u32[]{:S(2)}, u32[]{:S(2)}) %collective-permute-start.5) | collective-permute-done | bytes 557088 | tf_op jit(solution)/shard_map/ppermute | solution.py:19
  110.1 6.2 %collective-permute-start.7 = (bf16[128,2176]{1,0:T(8,128)(2,1)S(1)}, bf16[128,2176]{1,0:T(8,128)(2,1)S(1)}, u32[]{:S(2)}, u32[]{:S(2)}) collective-permute-start(bf16[128,2176]{1,0:T(8,128)(2,1)S(1)} %collective-permute-done.5.refs_6_), channel_id=1, source_target_pairs={{2,0},{3,1},{4,2},{5,3},{6,4},{7,5},{8,6},{9,7},{10,8},{11,9},{12,... | collective-permute-start | bytes 1671176 | tf_op jit(solution)/shard_map/ppermute | solution.py:19
  116.3 1.9 %collective-permute-start.6 = (bf16[128,2176]{1,0:T(8,128)(2,1)S(1)}, bf16[128,2176]{1,0:T(8,128)(2,1)S(1)}, u32[]{:S(2)}, u32[]{:S(2)}) collective-permute-start(bf16[128,2176]{1,0:T(8,128)(2,1)S(1)} %collective-permute-done.4.refs_5_), channel_id=1, source_target_pairs={{0,2},{1,3},{2,4},{3,5},{4,6},{5,7},{6,8},{7,9},{8,10},{9,11},{10,... | collective-permute-start | bytes 1671176 | tf_op jit(solution)/shard_map/ppermute | solution.py:19
  120.0 11.6 %collective-permute-done.6.refs_7_ = bf16[128,2176]{1,0:T(8,128)(2,1)S(1)} collective-permute-done((bf16[128,2176]{1,0:T(8,128)(2,1)S(1)}, bf16[128,2176]{1,0:T(8,128)(2,1)S(1)}, u32[]{:S(2)}, u32[]{:S(2)}) %collective-permute-start.6) | collective-permute-done | bytes 557088 | tf_op jit(solution)/shard_map/ppermute | solution.py:19
  133.4 3.8 %collective-permute-start.8 = (bf16[9,128,2176]{2,1,0:T(8,128)(2,1)}, bf16[9,128,2176]{2,1,0:T(8,128)(2,1)}, u32[]{:S(2)}, u32[]{:S(2)}) collective-permute-start(bf16[9,128,2176]{2,1,0:T(8,128)(2,1)} %bitcast_dynamic-update-slice_fusion), channel_id=1, source_target_pairs={{0,1},{1,0},{2,3},{3,2},{4,5},{5,4},{6,7},{7,6},{8,9},{9,8},{10,11... | collective-permute-start | bytes 15040520 | tf_op jit(solution)/shard_map/ppermute | solution.py:172
  140.5 1.4 compare_reduce_fusion
  141.8 1.2 pad_add_fusion.1.meta_ref
  143.0 2.9 %copy.24 = bf16[128,64,128]{0,2,1:T(8,128)(2,1)} copy(bf16[128,64,128]{2,1,0:T(8,128)(2,1)S(1)} %all-to-all-done) | data formatting | bytes 4194304 | tf_op jit(solution)/shard_map/all_to_all | solution.py:145
  146.0 43.1 %shard_map.77 = (bf16[128,8192]{1,0:T(8,128)(2,1)}, f32[128,128]{1,0:T(8,128)}) custom-call(s32[19]{0:T(128)} %pad_add_fusion.1.meta_ref, bf16[64,128,128]{2,1,0:T(8,128)(2,1)} %bitcast.48, bf16[9,128,2176]{2,1,0:T(8,128)(2,1)} %collective-permute-done.8.stack_ref, bf16[128,2176]{1,0:T(8,128)(2,1)} %copy-done.1, bf16[128,2176]{1,0:T(8,128)(2,1)} %copy-done.3, ...), custom_call_target="tpu_custom_call" | custom-call | tf_op jit(solution)/shard_map/pallas_call | solution.py:115
  (62 shorter events, 15.0 us)
Async XLA Ops:
  0.6 189.4 %copy-start = (bf16[8192,16]{0,1:T(8,128)(2,1)S(1)}, bf16[8192,16]{0,1:T(8,128)(2,1)}, u32[]{:S(2)}) copy-start(bf16[8192,16]{0,1:T(8,128)(2,1)} %param.12) | copy-start | bytes 786436
  3.6 22.8 %all-to-all-start.1 = ((bf16[128,16,128]{2,1,0:T(8,128)(2,1)}), bf16[128,16,128]{2,1,0:T(8,128)(2,1)S(1)}, u32[]{:S(2)}, u32[]{:S(2)}) async-start(bf16[128,16,128]{2,1,0:T(8,128)(2,1)} %pad_maximum_fusion), calls=%async_computation.1 | async-start | bytes 1048576 | tf_op jit(solution)/shard_map/all_to_all | solution.py:148
  26.3 34.8 %all-to-all-start = ((bf16[128,64,128]{2,1,0:T(8,128)(2,1)}), bf16[128,64,128]{2,1,0:T(8,128)(2,1)S(1)}, u32[]{:S(2)}, u32[]{:S(2)}) async-start(bf16[128,64,128]{2,1,0:T(8,128)(2,1)} %copy.23), calls=%async_computation | async-start | bytes 4194304 | tf_op jit(solution)/shard_map/all_to_all | solution.py:145
  61.4 72.1 %copy-start.1 = (bf16[128,2176]{1,0:T(8,128)(2,1)}, bf16[128,2176]{1,0:T(8,128)(2,1)S(1)}, u32[]{:S(2)}) copy-start(bf16[128,2176]{1,0:T(8,128)(2,1)S(1)} %fusion.1.refs_0_) | copy-start | bytes 1671172
  61.4 75.9 %copy-start.10 = (s32[32]{0:T(128)S(1)}, s32[32]{0:T(128)}, u32[]{:S(2)}) copy-start(s32[32]{0:T(128)} %param.11) | copy-start | bytes 388
  61.4 76.8 %copy-start.11 = (s32[9]{0:T(128)S(1)}, s32[9]{0:T(128)}, u32[]{:S(2)}) copy-start(s32[9]{0:T(128)} %constant.74.clone) | copy-start | bytes 112
  61.4 15.0 %collective-permute-start.1 = (bf16[128,2176]{1,0:T(8,128)(2,1)S(1)}, bf16[128,2176]{1,0:T(8,128)(2,1)S(1)}, u32[]{:S(2)}, u32[]{:S(2)}) collective-permute-start(bf16[128,2176]{1,0:T(8,128)(2,1)S(1)} %fusion.1.refs_0_), channel_id=1, source_target_pairs={{2,0},{3,1},{4,2},{5,3},{6,4},{7,5},{8,6},{9,7},{10,8},{11,9},{12,... | collective-permute-start | bytes 1671176 | tf_op jit(solution)/shard_map/ppermute | solution.py:19
  64.5 18.1 %collective-permute-start = (bf16[128,2176]{1,0:T(8,128)(2,1)S(1)}, bf16[128,2176]{1,0:T(8,128)(2,1)S(1)}, u32[]{:S(2)}, u32[]{:S(2)}) collective-permute-start(bf16[128,2176]{1,0:T(8,128)(2,1)S(1)} %fusion.1.refs_0_), channel_id=1, source_target_pairs={{0,2},{1,3},{2,4},{3,5},{4,6},{5,7},{6,8},{7,9},{8,10},{9,11},{10,... | collective-permute-start | bytes 1671176 | tf_op jit(solution)/shard_map/ppermute | solution.py:19
  76.4 60.8 %copy-start.2 = (bf16[128,2176]{1,0:T(8,128)(2,1)}, bf16[128,2176]{1,0:T(8,128)(2,1)S(1)}, u32[]{:S(2)}) copy-start(bf16[128,2176]{1,0:T(8,128)(2,1)S(1)} %collective-permute-done.1.refs_2_) | copy-start | bytes 1671172
  76.4 17.3 %collective-permute-start.3 = (bf16[128,2176]{1,0:T(8,128)(2,1)S(1)}, bf16[128,2176]{1,0:T(8,128)(2,1)S(1)}, u32[]{:S(2)}, u32[]{:S(2)}) collective-permute-start(bf16[128,2176]{1,0:T(8,128)(2,1)S(1)} %collective-permute-done.1.refs_2_), channel_id=1, source_target_pairs={{2,0},{3,1},{4,2},{5,3},{6,4},{7,5},{8,6},{9,7},{10,8},{11,9},{12,... | collective-permute-start | bytes 1671176 | tf_op jit(solution)/shard_map/ppermute | solution.py:19
  82.6 54.6 %copy-start.3 = (bf16[128,2176]{1,0:T(8,128)(2,1)}, bf16[128,2176]{1,0:T(8,128)(2,1)S(1)}, u32[]{:S(2)}) copy-start(bf16[128,2176]{1,0:T(8,128)(2,1)S(1)} %collective-permute-done.refs_1_) | copy-start | bytes 1671172
  82.6 17.2 %collective-permute-start.2 = (bf16[128,2176]{1,0:T(8,128)(2,1)S(1)}, bf16[128,2176]{1,0:T(8,128)(2,1)S(1)}, u32[]{:S(2)}, u32[]{:S(2)}) collective-permute-start(bf16[128,2176]{1,0:T(8,128)(2,1)S(1)} %collective-permute-done.refs_1_), channel_id=1, source_target_pairs={{0,2},{1,3},{2,4},{3,5},{4,6},{5,7},{6,8},{7,9},{8,10},{9,11},{10,... | collective-permute-start | bytes 1671176 | tf_op jit(solution)/shard_map/ppermute | solution.py:19
  93.6 43.6 %copy-start.4 = (bf16[128,2176]{1,0:T(8,128)(2,1)}, bf16[128,2176]{1,0:T(8,128)(2,1)S(1)}, u32[]{:S(2)}) copy-start(bf16[128,2176]{1,0:T(8,128)(2,1)S(1)} %collective-permute-done.3.refs_4_) | copy-start | bytes 1671172
  93.6 16.4 %collective-permute-start.5 = (bf16[128,2176]{1,0:T(8,128)(2,1)S(1)}, bf16[128,2176]{1,0:T(8,128)(2,1)S(1)}, u32[]{:S(2)}, u32[]{:S(2)}) collective-permute-start(bf16[128,2176]{1,0:T(8,128)(2,1)S(1)} %collective-permute-done.3.refs_4_), channel_id=1, source_target_pairs={{2,0},{3,1},{4,2},{5,3},{6,4},{7,5},{8,6},{9,7},{10,8},{11,9},{12,... | collective-permute-start | bytes 1671176 | tf_op jit(solution)/shard_map/ppermute | solution.py:19
  99.9 37.3 %copy-start.5 = (bf16[128,2176]{1,0:T(8,128)(2,1)}, bf16[128,2176]{1,0:T(8,128)(2,1)S(1)}, u32[]{:S(2)}) copy-start(bf16[128,2176]{1,0:T(8,128)(2,1)S(1)} %collective-permute-done.2.refs_3_) | copy-start | bytes 1671172
  99.9 16.4 %collective-permute-start.4 = (bf16[128,2176]{1,0:T(8,128)(2,1)S(1)}, bf16[128,2176]{1,0:T(8,128)(2,1)S(1)}, u32[]{:S(2)}, u32[]{:S(2)}) collective-permute-start(bf16[128,2176]{1,0:T(8,128)(2,1)S(1)} %collective-permute-done.2.refs_3_), channel_id=1, source_target_pairs={{0,2},{1,3},{2,4},{3,5},{4,6},{5,7},{6,8},{7,9},{8,10},{9,11},{10,... | collective-permute-start | bytes 1671176 | tf_op jit(solution)/shard_map/ppermute | solution.py:19
  110.1 27.2 %copy-start.6 = (bf16[128,2176]{1,0:T(8,128)(2,1)}, bf16[128,2176]{1,0:T(8,128)(2,1)S(1)}, u32[]{:S(2)}) copy-start(bf16[128,2176]{1,0:T(8,128)(2,1)S(1)} %collective-permute-done.5.refs_6_) | copy-start | bytes 1671172
  110.1 22.5 %collective-permute-start.7 = (bf16[128,2176]{1,0:T(8,128)(2,1)S(1)}, bf16[128,2176]{1,0:T(8,128)(2,1)S(1)}, u32[]{:S(2)}, u32[]{:S(2)}) collective-permute-start(bf16[128,2176]{1,0:T(8,128)(2,1)S(1)} %collective-permute-done.5.refs_6_), channel_id=1, source_target_pairs={{2,0},{3,1},{4,2},{5,3},{6,4},{7,5},{8,6},{9,7},{10,8},{11,9},{12,... | collective-permute-start | bytes 1671176 | tf_op jit(solution)/shard_map/ppermute | solution.py:19
  116.3 21.0 %copy-start.7 = (bf16[128,2176]{1,0:T(8,128)(2,1)}, bf16[128,2176]{1,0:T(8,128)(2,1)S(1)}, u32[]{:S(2)}) copy-start(bf16[128,2176]{1,0:T(8,128)(2,1)S(1)} %collective-permute-done.4.refs_5_) | copy-start | bytes 1671172
  116.3 15.3 %collective-permute-start.6 = (bf16[128,2176]{1,0:T(8,128)(2,1)S(1)}, bf16[128,2176]{1,0:T(8,128)(2,1)S(1)}, u32[]{:S(2)}, u32[]{:S(2)}) collective-permute-start(bf16[128,2176]{1,0:T(8,128)(2,1)S(1)} %collective-permute-done.4.refs_5_), channel_id=1, source_target_pairs={{0,2},{1,3},{2,4},{3,5},{4,6},{5,7},{6,8},{7,9},{8,10},{9,11},{10,... | collective-permute-start | bytes 1671176 | tf_op jit(solution)/shard_map/ppermute | solution.py:19
  131.6 5.7 %copy-start.9 = (bf16[128,2176]{1,0:T(8,128)(2,1)}, bf16[128,2176]{1,0:T(8,128)(2,1)S(1)}, u32[]{:S(2)}) copy-start(bf16[128,2176]{1,0:T(8,128)(2,1)S(1)} %collective-permute-done.6.refs_7_) | copy-start | bytes 1671172
  132.5 4.7 %copy-start.8 = (bf16[128,2176]{1,0:T(8,128)(2,1)}, bf16[128,2176]{1,0:T(8,128)(2,1)S(1)}, u32[]{:S(2)}) copy-start(bf16[128,2176]{1,0:T(8,128)(2,1)S(1)} %collective-permute-done.7.refs_8_) | copy-start | bytes 1671172
  133.4 12.5 %collective-permute-start.8 = (bf16[9,128,2176]{2,1,0:T(8,128)(2,1)}, bf16[9,128,2176]{2,1,0:T(8,128)(2,1)}, u32[]{:S(2)}, u32[]{:S(2)}) collective-permute-start(bf16[9,128,2176]{2,1,0:T(8,128)(2,1)} %bitcast_dynamic-update-slice_fusion), channel_id=1, source_target_pairs={{0,1},{1,0},{2,3},{3,2},{4,5},{5,4},{6,7},{7,6},{8,9},{9,8},{10,11... | collective-permute-start | bytes 15040520 | tf_op jit(solution)/shard_map/ppermute | solution.py:172
